TPU v7x, 512 devices: a whole 4x4x16 slice. The times are simulated.
512 devices in a mesh: dp: 32 (over y, z_hi, x), tensor: 16 (over z_lo, core).
Axes of the slice: x: 4, y: 4, z: 16 (z_hi: 2, z_lo: 8; z = z_hi * 8 + z_lo), core: 2. Of those that a mesh axis runs over, the one named last changes fastest.
Arguments:
- inner_x: bfloat16 [32768, 8192], P(('dp', 'tensor')), parts along dimension 0, may hold values from -6 to 6
- inner_bc: bfloat16 [32768, 2048], P(('dp', 'tensor')), parts along dimension 0, may hold values from -6 to 6
- step_raw: bfloat16 [32768, 128], P(('dp', 'tensor')), parts along dimension 0, may hold values from -5 to 5
- conv_state_x: bfloat16 [96, 8192], P('dp', 'tensor'), parts along dimension 0, may hold values from -6 to 6
- conv_state_bc: bfloat16 [96, 2048], P('dp'), parts along dimension 0, may hold values from -6 to 6
- conv_weight_x: bfloat16 [4, 8192], P(None, 'tensor'), may hold values from -3 to 3
- conv_bias_x: bfloat16 [8192], P('tensor'), may hold values from -3 to 3
- conv_weight_bc: bfloat16 [4, 2048], replicated, may hold values from -3 to 3
- conv_bias_bc: bfloat16 [2048], replicated, may hold values from -3 to 3
- step_bias: float32 [128], P('tensor'), may hold values from -4 to -2
- decay_rate: float32 [128], P('tensor'), may hold values from 0 to 1, as said below
- skip_gain: float32 [128], P('tensor'), may hold values from 0.5 to 1.5
- norm_weight: bfloat16 [8192], replicated, may hold values from 0.5 to 1.5
- scan_state: float32 [4096, 64, 256], P(('dp', 'tensor')), parts along dimension 0, may hold values from -3 to 3
Outputs:
- normed: bfloat16 [32768, 8192], P(('dp', 'tensor')), parts along dimension 0
- final_state: float32 [4096, 64, 256], P(('dp', 'tensor')), parts along dimension 0
- conv_tail_x: bfloat16 [96, 8192], P('dp', 'tensor'), parts along dimension 0
- conv_tail_bc: bfloat16 [96, 2048], P('dp', 'tensor'), parts along dimension 0
There are 32 independent parts, one for each index of `dp`. A program takes and returns all parts, laid end to end along the dimension named above; an argument that names none is the same for every part. Nothing has to cross between parts.
Inputs may be any that keep to these rules, and one draw needn't show every extreme that they name: decay_rate lies between 2 / 1024 and 1 / 2.
All inputs are finite; a program needn't handle non-finite values.
Results may differ from a plain program's by a relative error of at most 0.0051.
Values may be sent and summed in bfloat16 or wider, within the bound.
No kernel may reach another device: no remote copies, remote signals or barrier semaphores. Data moves between devices by JAX's collectives and lax.ppermute only.
A program may use at most 64 MiB of HBM per device.

v0:
```python
import functools
import jax
import jax.numpy as jnp
from jax import lax
import numpy as np
from jax.sharding import Mesh, PartitionSpec as P

HEAD_DIM = 64
STATE = 256
GROUPS = 4
CONV_K = 4
INNER = 8192
EPSILON = 1e-05
TENSOR = ("tg", "tj")


def causal_conv(raw, state, weight, bias):
    length = raw.shape[0]
    padded = jnp.concatenate([state.astype(jnp.float32), raw.astype(jnp.float32)], axis=0)
    total = jnp.zeros(raw.shape, jnp.float32) + bias.astype(jnp.float32)[None, :]
    for kernel_tap in range(CONV_K):
        total = (
            total
            + weight[kernel_tap].astype(jnp.float32)[None, :]
            * padded[kernel_tap : kernel_tap + length]
        )
    return jax.nn.silu(total).astype(jnp.bfloat16)


def state_mix(
    mixed_x, mixed_bc, step_raw, step_bias, decay_rate, skip_gain, scan_state, groups_here
):
    length = mixed_x.shape[0]
    heads_here = step_raw.shape[1]
    per_group = heads_here // groups_here
    step_size = jax.nn.softplus(step_raw.astype(jnp.float32) + step_bias[None, :])
    running = jnp.cumsum(-step_size * decay_rate[None, :], axis=0)
    halves = mixed_bc.reshape(length, groups_here, 2, STATE)
    input_map = halves[:, :, 0, :]
    output_map = halves[:, :, 1, :]
    step_cols = jnp.transpose(step_size)
    running_cols = jnp.transpose(running)
    query_rows = min(512, length)
    pieces = []
    for row_start in range(0, length, query_rows):
        row_stop = row_start + query_rows
        scores = jnp.einsum(
            "tgn,sgn->gts",
            output_map[row_start:row_stop],
            input_map[:row_stop],
            preferred_element_type=jnp.float32,
        )
        causal = row_start + lax.broadcasted_iota(
            jnp.int32, (query_rows, row_stop), 0
        ) >= lax.broadcasted_iota(jnp.int32, (query_rows, row_stop), 1)
        visible = mixed_x[:row_stop]

        def one_head(
            item,
            scores=scores,
            causal=causal,
            visible=visible,
            row_start=row_start,
            row_stop=row_stop,
        ):
            head_index, step_head, running_head = item
            group_scores = lax.dynamic_index_in_dim(
                scores, head_index // per_group, 0, keepdims=False
            )
            log_gap = running_head[row_start:row_stop, None] - running_head[None, :row_stop]
            decayed = jnp.exp(jnp.where(causal, log_gap, 0.0))
            weights = jnp.where(
                causal, group_scores * decayed * step_head[None, :row_stop], 0.0
            ).astype(jnp.bfloat16)
            values = lax.dynamic_slice_in_dim(visible, head_index * HEAD_DIM, HEAD_DIM, 1)
            return jnp.dot(weights, values, preferred_element_type=jnp.float32)

        local_mix = lax.map(
            one_head, (jnp.arange(heads_here, dtype=jnp.int32), step_cols, running_cols)
        )
        pieces.append(
            jnp.transpose(local_mix, (1, 0, 2)).reshape(query_rows, heads_here * HEAD_DIM)
        )
    local_all = jnp.concatenate(pieces, axis=0)
    grouped_state = scan_state.reshape(groups_here, per_group, HEAD_DIM, STATE)
    carried = jnp.einsum(
        "tgn,ghpn->tghp",
        output_map.astype(jnp.float32),
        grouped_state,
        precision=lax.Precision.HIGHEST,
    )
    carried = carried.reshape(length, heads_here, HEAD_DIM) * jnp.exp(running)[:, :, None]
    channels = mixed_x.reshape(length, heads_here, HEAD_DIM).astype(jnp.float32)
    mixed = (
        local_all.reshape(length, heads_here, HEAD_DIM)
        + carried
        + skip_gain[None, :, None] * channels
    )
    mixed_y = mixed.reshape(length, heads_here * HEAD_DIM).astype(jnp.bfloat16)
    tail_decay = jnp.exp(running[length - 1][None, :] - running) * step_size
    weighted = (
        input_map.astype(jnp.float32)[:, :, None, :]
        * tail_decay.reshape(length, groups_here, per_group)[:, :, :, None]
    ).astype(jnp.bfloat16)
    gathered_in = jnp.einsum(
        "tghp,tghn->ghpn",
        mixed_x.reshape(length, groups_here, per_group, HEAD_DIM),
        weighted,
        preferred_element_type=jnp.float32,
    )
    final = (
        jnp.exp(running[length - 1]).reshape(groups_here, per_group)[:, :, None, None]
        * grouped_state
        + gathered_in
    )
    return (mixed_y, final.reshape(heads_here, HEAD_DIM, STATE))


def group_norm(mixed_y, norm_weight):
    rows = mixed_y.shape[0]
    values = mixed_y.astype(jnp.float32).reshape(rows, GROUPS, INNER // GROUPS)
    mean_square = jnp.mean(values * values, axis=2, keepdims=True)
    scaled = (values * lax.rsqrt(mean_square + EPSILON)).reshape(rows, INNER)
    return (scaled * norm_weight.astype(jnp.float32)[None, :]).astype(jnp.bfloat16)


def local(
    inner_x,
    inner_bc,
    step_raw,
    conv_state_x,
    conv_state_bc,
    conv_weight_x,
    conv_bias_x,
    conv_weight_bc,
    conv_bias_bc,
    step_bias,
    decay_rate,
    skip_gain,
    norm_weight,
    scan_state,
    *,
    group_size,
    tensor_count
):
    device_rank = lax.axis_index("tg") * group_size + lax.axis_index("tj")
    token_rows = inner_x.shape[0]
    heads_here = step_bias.shape[0]
    x_width = heads_here * HEAD_DIM
    bc_width = inner_bc.shape[1] // tensor_count
    x_send = jnp.transpose(inner_x.reshape(token_rows, tensor_count, x_width), (1, 0, 2))
    bc_send = jnp.transpose(inner_bc.reshape(token_rows, tensor_count, bc_width), (1, 0, 2))
    step_send = jnp.transpose(step_raw.reshape(token_rows, tensor_count, heads_here), (1, 0, 2))
    send = jnp.concatenate(
        [
            x_send.reshape(tensor_count, -1),
            bc_send.reshape(tensor_count, -1),
            step_send.reshape(tensor_count, -1),
        ],
        axis=1,
    )
    recv = lax.all_to_all(send, TENSOR, 0, 0, tiled=True)
    length = tensor_count * token_rows
    x_end = token_rows * x_width
    bc_end = x_end + token_rows * bc_width
    head_x = recv[:, :x_end].reshape(length, x_width)
    head_bc_part = recv[:, x_end:bc_end].reshape(length, bc_width)
    head_step = recv[:, bc_end:].reshape(length, heads_here)
    column_start = device_rank * bc_width
    own_state_bc = lax.dynamic_slice_in_dim(conv_state_bc, column_start, bc_width, 1)
    own_weight_bc = lax.dynamic_slice_in_dim(conv_weight_bc, column_start, bc_width, 1)
    own_bias_bc = lax.dynamic_slice_in_dim(conv_bias_bc, column_start, bc_width, 0)
    mixed_bc_part = causal_conv(head_bc_part, own_state_bc, own_weight_bc, own_bias_bc)
    mixed_bc = lax.all_gather(mixed_bc_part, "tj", axis=1, tiled=True)
    mixed_x = causal_conv(head_x, conv_state_x, conv_weight_x, conv_bias_x)
    mixed_y, final_state = state_mix(
        mixed_x, mixed_bc, head_step, step_bias, decay_rate, skip_gain, scan_state, 1
    )
    token_y = lax.all_to_all(mixed_y, TENSOR, split_axis=0, concat_axis=1, tiled=True)
    normed = group_norm(token_y, norm_weight)
    tail_x = head_x[length - CONV_K + 1 :]
    tail_bc = head_bc_part[length - CONV_K + 1 :]
    return (normed, final_state, tail_x, tail_bc)


def solution(mesh):
    dp_count = mesh.shape["dp"]
    tensor_count = mesh.shape["tensor"]
    group_size = tensor_count // GROUPS
    grouped = Mesh(
        np.asarray(mesh.devices).reshape(dp_count, GROUPS, group_size), ("dp", "tg", "tj")
    )
    rows = ("dp",) + TENSOR
    return jax.shard_map(
        functools.partial(local, group_size=group_size, tensor_count=tensor_count),
        mesh=grouped,
        in_specs=(
            P(rows, None),
            P(rows, None),
            P(rows, None),
            P("dp", TENSOR),
            P("dp", None),
            P(None, TENSOR),
            P(TENSOR),
            P(),
            P(),
            P(TENSOR),
            P(TENSOR),
            P(TENSOR),
            P(),
            P(rows, None, None),
        ),
        out_specs=(P(rows, None), P(rows, None, None), P("dp", TENSOR), P("dp", TENSOR)),
        check_vma=False,
    )
```

profile of v0, /device:TPU:65, one launch (start us, length us, event | category | flops | bytes accessed | tf_op | source)
XLA Modules:
  0.0 247.7 jit_solution(4635555850143321165)
XLA Ops:
  7.2 0.9 copy.152
  9.9 1.7 reduce.7
  11.7 1.3 reshape.197
  12.9 12.5 %all-to-all-start = ((bf16[16,2,20736]{2,1,0:T(2,128)(2,1)}), bf16[16,2,20736]{2,1,0:T(2,128)(2,1)}, u32[]{:S(2)}, u32[]{:S(2)}) async-start(bf16[16,2,20736]{2,1,0:T(2,128)(2,1)} %reshape.197), calls=%async_computation | async-start | bytes 2654208 | tf_op jit(solution)/shard_map/all_to_all | solution.py:162
  25.6 0.8 dynamic-slice_convert_fusion.1
  26.4 0.7 constant_dynamic-slice_fusion.4
  27.1 0.7 dynamic-slice_convert_fusion
  27.8 58.0 %all-to-all-done = bf16[16,2,20736]{2,1,0:T(2,128)(2,1)} async-done(((bf16[16,2,20736]{2,1,0:T(2,128)(2,1)}), bf16[16,2,20736]{2,1,0:T(2,128)(2,1)}, u32[]{:S(2)}, u32[]{:S(2)}) %all-to-all-start) | async-done | bytes 1327136 | tf_op jit(solution)/shard_map/all_to_all | solution.py:162
  85.7 4.4 %reshape.198 = bf16[16,1,41472]{2,1,0:T(2,128)(2,1)S(1)} reshape(bf16[16,2,20736]{2,1,0:T(2,128)(2,1)} %all-to-all-done) | data formatting | bytes 2654208
  90.3 1.1 copy-done.5
  91.6 1.1 multiply_convert_fusion.6
  92.8 1.0 slice.147
  93.8 1.6 reshape.178
  96.1 2.3 reduce-window.6
  99.0 1.4 multiply_convert_fusion.3
  101.0 1.8 copy.163
  102.8 15.7 %all-gather.2.cloned.1.call-done = bf16[1024,512]{1,0:T(8,128)(2,1)} async-done(((bf16[1024,128]{1,0:T(8,128)(2,1)}), bf16[1024,512]{1,0:T(8,128)(2,1)}) %all-gather.2.cloned.1.call-update) | async-done | bytes 1048592 | tf_op jit(solution)/shard_map/all_gather | solution.py:174
  118.6 1.5 copy.156
  120.4 1.8 convolution_bitcast_fusion.2
  122.3 13.6 %while.24 = (s32[]{:T(128)}, f32[8,512,64]{1,2,0:T(8,128)S(1)}, f32[1,512,512]{2,1,0:T(8,128)S(1)}, f32[8,1024]{1,0:T(8,128)S(1)}, f32[8,1024]{1,0:T(8,128)S(1)}...) while((s32[]{:T(128)}, f32[8,512,64]{1,2,0:T(8,128)S(1)}, ...), condition=%wide.region_3.4_spmd.clone.clone, body=%wide.region_2.3_spmd.clone.clone.sunk | while | flops 35389444 | bytes 1325243 | solution.py:78
  122.3 0.6 dynamic_slice.73
  124.0 0.6 dynamic_slice.73
  127.4 0.6 dynamic_slice.73
  129.1 0.6 dynamic_slice.73
  130.8 0.6 dynamic_slice.73
  135.9 1.3 copy.159
  137.4 30.9 %while.25 = (s32[]{:T(128)}, f32[8,512,64]{1,2,0:T(8,128)S(1)}, f32[1,512,1024]{2,1,0:T(8,128)}, f32[8,1024]{1,0:T(8,128)S(1)}, f32[8,1024]{1,0:T(8,128)S(1)}, /...) while((s32[]{:T(128)}, f32[8,512,64]{1,2,0:T(8,128)S(1)}, ...), condition=%wide.region_5.6_spmd.clone.clone, body=%wide.region_4.5_spmd.clone.clone.sunk | while | flops 70778888 | bytes 2523355 | solution.py:78
  138.7 2.5 %fusion.71 = f32[8,512,64]{1,2,0:T(8,128)S(1)} fusion(f32[8,512,64]{1,2,0:T(8,128)S(1)} %get-tuple-element.426, s32[]{:T(128)S(6)} %copy.197, f32[1,512,1024]{2,1,0:T(8,128)} %get-tuple-element.440, s32[512]{0:T(512)S(1)} %get-tuple-element.445, f32[1024]{0:T(1024)S(1)} %bitcast.197, f32[1024]{0:T(1024)S(1)} %bitcast.198, f32[512]{0:T(512)S(1)} %bitcast.201, ...), kind=kOutput, calls=%fused_computation.28.clone.1 | convolution fusion | flops 70778880 | bytes 2502664 | tf_op jit(solution)/shard_map/while/body/eval_jaxpr/dot_general | solution.py:76
  142.6 2.5 %fusion.71 = f32[8,512,64]{1,2,0:T(8,128)S(1)} fusion(f32[8,512,64]{1,2,0:T(8,128)S(1)} %get-tuple-element.426, s32[]{:T(128)S(6)} %copy.197, f32[1,512,1024]{2,1,0:T(8,128)} %get-tuple-element.440, s32[512]{0:T(512)S(1)} %get-tuple-element.445, f32[1024]{0:T(1024)S(1)} %bitcast.197, f32[1024]{0:T(1024)S(1)} %bitcast.198, f32[512]{0:T(512)S(1)} %bitcast.201, ...), kind=kOutput, calls=%fused_computation.28.clone.1 | convolution fusion | flops 70778880 | bytes 2502664 | tf_op jit(solution)/shard_map/while/body/eval_jaxpr/dot_general | solution.py:76
  146.5 2.5 %fusion.71 = f32[8,512,64]{1,2,0:T(8,128)S(1)} fusion(f32[8,512,64]{1,2,0:T(8,128)S(1)} %get-tuple-element.426, s32[]{:T(128)S(6)} %copy.197, f32[1,512,1024]{2,1,0:T(8,128)} %get-tuple-element.440, s32[512]{0:T(512)S(1)} %get-tuple-element.445, f32[1024]{0:T(1024)S(1)} %bitcast.197, f32[1024]{0:T(1024)S(1)} %bitcast.198, f32[512]{0:T(512)S(1)} %bitcast.201, ...), kind=kOutput, calls=%fused_computation.28.clone.1 | convolution fusion | flops 70778880 | bytes 2502664 | tf_op jit(solution)/shard_map/while/body/eval_jaxpr/dot_general | solution.py:76
  150.3 2.5 %fusion.71 = f32[8,512,64]{1,2,0:T(8,128)S(1)} fusion(f32[8,512,64]{1,2,0:T(8,128)S(1)} %get-tuple-element.426, s32[]{:T(128)S(6)} %copy.197, f32[1,512,1024]{2,1,0:T(8,128)} %get-tuple-element.440, s32[512]{0:T(512)S(1)} %get-tuple-element.445, f32[1024]{0:T(1024)S(1)} %bitcast.197, f32[1024]{0:T(1024)S(1)} %bitcast.198, f32[512]{0:T(512)S(1)} %bitcast.201, ...), kind=kOutput, calls=%fused_computation.28.clone.1 | convolution fusion | flops 70778880 | bytes 2502664 | tf_op jit(solution)/shard_map/while/body/eval_jaxpr/dot_general | solution.py:76
  154.2 2.5 %fusion.71 = f32[8,512,64]{1,2,0:T(8,128)S(1)} fusion(f32[8,512,64]{1,2,0:T(8,128)S(1)} %get-tuple-element.426, s32[]{:T(128)S(6)} %copy.197, f32[1,512,1024]{2,1,0:T(8,128)} %get-tuple-element.440, s32[512]{0:T(512)S(1)} %get-tuple-element.445, f32[1024]{0:T(1024)S(1)} %bitcast.197, f32[1024]{0:T(1024)S(1)} %bitcast.198, f32[512]{0:T(512)S(1)} %bitcast.201, ...), kind=kOutput, calls=%fused_computation.28.clone.1 | convolution fusion | flops 70778880 | bytes 2502664 | tf_op jit(solution)/shard_map/while/body/eval_jaxpr/dot_general | solution.py:76
  158.1 2.5 %fusion.71 = f32[8,512,64]{1,2,0:T(8,128)S(1)} fusion(f32[8,512,64]{1,2,0:T(8,128)S(1)} %get-tuple-element.426, s32[]{:T(128)S(6)} %copy.197, f32[1,512,1024]{2,1,0:T(8,128)} %get-tuple-element.440, s32[512]{0:T(512)S(1)} %get-tuple-element.445, f32[1024]{0:T(1024)S(1)} %bitcast.197, f32[1024]{0:T(1024)S(1)} %bitcast.198, f32[512]{0:T(512)S(1)} %bitcast.201, ...), kind=kOutput, calls=%fused_computation.28.clone.1 | convolution fusion | flops 70778880 | bytes 2502664 | tf_op jit(solution)/shard_map/while/body/eval_jaxpr/dot_general | solution.py:76
  161.9 2.5 %fusion.71 = f32[8,512,64]{1,2,0:T(8,128)S(1)} fusion(f32[8,512,64]{1,2,0:T(8,128)S(1)} %get-tuple-element.426, s32[]{:T(128)S(6)} %copy.197, f32[1,512,1024]{2,1,0:T(8,128)} %get-tuple-element.440, s32[512]{0:T(512)S(1)} %get-tuple-element.445, f32[1024]{0:T(1024)S(1)} %bitcast.197, f32[1024]{0:T(1024)S(1)} %bitcast.198, f32[512]{0:T(512)S(1)} %bitcast.201, ...), kind=kOutput, calls=%fused_computation.28.clone.1 | convolution fusion | flops 70778880 | bytes 2502664 | tf_op jit(solution)/shard_map/while/body/eval_jaxpr/dot_general | solution.py:76
  165.8 2.5 %fusion.71 = f32[8,512,64]{1,2,0:T(8,128)S(1)} fusion(f32[8,512,64]{1,2,0:T(8,128)S(1)} %get-tuple-element.426, s32[]{:T(128)S(6)} %copy.197, f32[1,512,1024]{2,1,0:T(8,128)} %get-tuple-element.440, s32[512]{0:T(512)S(1)} %get-tuple-element.445, f32[1024]{0:T(1024)S(1)} %bitcast.197, f32[1024]{0:T(1024)S(1)} %bitcast.198, f32[512]{0:T(512)S(1)} %bitcast.201, ...), kind=kOutput, calls=%fused_computation.28.clone.1 | convolution fusion | flops 70778880 | bytes 2502664 | tf_op jit(solution)/shard_map/while/body/eval_jaxpr/dot_general | solution.py:76
  168.3 1.3 copy.160
  169.6 2.2 fusion.52
  171.8 1.8 copy.162
  173.7 4.8 %fusion.42 = bf16[1024,512]{1,0:T(8,128)(2,1)} fusion(f32[512,512]{1,0:T(8,128)} %copy.160, f32[512,512]{1,0:T(8,128)} %copy.159, bf16[1024,512]{1,0:T(8,128)(2,1)S(1)} %get-tuple-element.485, f32[1024,512]{1,0:T(8,128)} %copy.162, f32[1024,512]{1,0:T(8,128)} %copy.163, f32[512]{0:T(512)S(1)} %mul.284), kind=kLoop, calls=%fused_computation.55 | loop fusion | flops 3670016 | bytes 8390656 | tf_op jit(solution)/shard_map/convert_element_type | solution.py:99
  178.4 10.2 %all-to-all-start.1 = ((bf16[16,64,512]{2,1,0:T(8,128)(2,1)}), bf16[16,64,512]{2,1,0:T(8,128)(2,1)S(1)}, u32[]{:S(2)}, u32[]{:S(2)}) async-start(bf16[16,64,512]{2,1,0:T(8,128)(2,1)} %bitcast.184), calls=%async_computation.1 | async-start | bytes 2097152 | tf_op jit(solution)/shard_map/all_to_all | solution.py:179
  188.7 1.2 slice.158
  189.9 1.3 slice.157
  191.2 1.3 copy.166
  192.6 1.3 copy.167
  193.9 3.8 %fusion.43 = f32[8,64,256]{2,1,0:T(8,128)} fusion(bf16[1024,8,64]{0,2,1:T(8,128)(2,1)} %bitcast.190, f32[1024,8]{0,1:T(8,128)S(1)} %get-tuple-element.299, f32[1024,256]{1,0:T(8,128)} %copy.167, f32[8,64,256]{2,1,0:T(8,128)S(1)} %copy-done.8, f32[8]{0:T(128)S(1)} %exp.35), kind=kOutput, calls=%fused_computation.62 | convolution fusion | flops 272891904 | bytes 3178528 | tf_op jit(solution)/shard_map/tghp,tghn->ghpn/dot_general | solution.py:105
  197.7 39.6 %all-to-all-done.1 = bf16[16,64,512]{2,1,0:T(8,128)(2,1)S(1)} async-done(((bf16[16,64,512]{2,1,0:T(8,128)(2,1)}), bf16[16,64,512]{2,1,0:T(8,128)(2,1)S(1)}, u32[]{:S(2)}, u32[]{:S(2)}) %all-to-all-start.1) | async-done | bytes 1048608 | tf_op jit(solution)/shard_map/all_to_all | solution.py:179
  238.5 1.2 copy.176
  239.7 1.2 multiply_convert_fusion.2
  (129 shorter events, 16.9 us)
Async XLA Ops:
  7.2 1.2 copy-start
  7.2 1.4 copy-start.10
  11.6 13.8 %copy-start.15 = (bf16[512]{0:T(512)(128)(2,1)S(1)}, bf16[512]{0:T(512)(128)(2,1)}, u32[]{:S(2)}) copy-start(bf16[512]{0:T(512)(128)(2,1)} %param.24) | copy-start | bytes 3076
  11.6 13.8 %copy-start.17 = (f32[8]{0:T(128)S(1)}, f32[8]{0:T(128)}, u32[]{:S(2)}) copy-start(f32[8]{0:T(128)} %param.29) | copy-start | bytes 100
  11.6 14.0 %copy-start.13 = (bf16[3,512]{1,0:T(4,128)(2,1)S(1)}, bf16[3,512]{1,0:T(4,128)(2,1)}, u32[]{:S(2)}) copy-start(bf16[3,512]{1,0:T(4,128)(2,1)} %param.21) | copy-start | bytes 9220
  11.6 16.1 %copy-start.12 = (bf16[4,512]{1,0:T(4,128)(2,1)S(1)}, bf16[4,512]{1,0:T(4,128)(2,1)}, u32[]{:S(2)}) copy-start(bf16[4,512]{1,0:T(4,128)(2,1)} %param.23) | copy-start | bytes 12292
  12.9 72.8 %all-to-all-start = ((bf16[16,2,20736]{2,1,0:T(2,128)(2,1)}), bf16[16,2,20736]{2,1,0:T(2,128)(2,1)}, u32[]{:S(2)}, u32[]{:S(2)}) async-start(bf16[16,2,20736]{2,1,0:T(2,128)(2,1)} %reshape.197), calls=%async_computation | async-start | bytes 2654208 | tf_op jit(solution)/shard_map/all_to_all | solution.py:162
  25.4 93.2 %all-gather.2.cloned.1.call-start = ((), (), s32[]{:S(2)}) async-start(), calls=%async_computation.2 | async-start | bytes 1310720 | tf_op jit(solution)/shard_map/all_gather | solution.py:174
  90.3 1.1 copy-start.5
  91.4 1.4 copy-start.6
  91.5 3.9 %copy-start.9 = (bf16[1024,128]{1,0:T(8,128)(2,1)}, bf16[1024,128]{1,0:T(8,128)(2,1)S(1)}, u32[]{:S(2)}) copy-start(bf16[1024,128]{1,0:T(8,128)(2,1)S(1)} %reshape.172) | copy-start | bytes 786436
  93.8 2.1 copy-start.14
  93.8 2.1 copy-start.16
  95.4 3.6 %copy-start.7 = (bf16[1024,512]{1,0:T(8,128)(2,1)}, bf16[1024,512]{1,0:T(8,128)(2,1)S(1)}, u32[]{:S(2)}) copy-start(bf16[1024,512]{1,0:T(8,128)(2,1)S(1)} %reshape.178) | copy-start | bytes 3145732
  100.4 2.4 copy-start.1
  120.1 2.1 copy-start.3
  120.4 1.9 slice-start
  135.9 1.5 copy-start.2
  178.4 10.2 %copy-start.11 = (bf16[8192]{0:T(1024)(128)(2,1)S(1)}, bf16[8192]{0:T(1024)(128)(2,1)}, u32[]{:S(2)}) copy-start(bf16[8192]{0:T(1024)(128)(2,1)} %param.30) | copy-start | bytes 49156
  178.4 14.0 %copy-start.4 = (bf16[1024,512]{0,1:T(8,128)(2,1)S(1)}, bf16[1024,512]{0,1:T(8,128)(2,1)}, u32[]{:S(2)}) copy-start(bf16[1024,512]{0,1:T(8,128)(2,1)} %copy-done.3) | copy-start | bytes 3145732
  178.4 58.8 %all-to-all-start.1 = ((bf16[16,64,512]{2,1,0:T(8,128)(2,1)}), bf16[16,64,512]{2,1,0:T(8,128)(2,1)S(1)}, u32[]{:S(2)}, u32[]{:S(2)}) async-start(bf16[16,64,512]{2,1,0:T(8,128)(2,1)} %bitcast.184), calls=%async_computation.1 | async-start | bytes 2097152 | tf_op jit(solution)/shard_map/all_to_all | solution.py:179
  192.6 1.3 copy-start.8
Sparse Core Ops, SparseCore 0:
  92.8 25.7 all-gather.1
where the time goes:
time: 249 us; the launch traced here: 248 us
  waiting for transfers between devices  113 us (45%)
  local copies, waits for them, and re-layouts  39.5 us (16%)
  matrix products  31.5 us (13%)
  starting transfers between devices  22.7 us (9%)
  other arithmetic  15.3 us (6%)
  between operations  14.5 us (6%)
  loops' own time  10.8 us (4%)
    all_to_all x1, waiting for transfers between devices, local(): recv = lax.all_to_all(send, TENSOR, 0, 0, tiled=True)  58 us
    all_to_all x1, waiting for transfers between devices, local(): lax.all_to_all(mixed_y, TENSOR, split_axis=0, concat_axis=1, tiled=True)  39.6 us
    dot_general x16, matrix products, one_head(): return jnp.dot(weights, values, preferred_element_type=jnp.float32)  23.5 us
    all_gather x1, waiting for transfers between devices, local(): mixed_bc = lax.all_gather(mixed_bc_part, 'tj', axis=1, tiled=True)  15.7 us
    all_to_all x1, starting transfers between devices, local(): recv = lax.all_to_all(send, TENSOR, 0, 0, tiled=True)  12.5 us
    another operation x2, loops' own time, state_mix(): lax.map(one_head, (jnp.arange(heads_here, dtype=jnp.int32), step_cols, ru...  10.8 us
    all_to_all x1, starting transfers between devices, local(): lax.all_to_all(mixed_y, TENSOR, split_axis=0, concat_axis=1, tiled=True)  10.2 us
    unnamed x44, local copies, waits for them, and re-layouts  9.96 us
  transfers between devices with their start and end apart: 3, of which 3 were waited for; matrix products, arithmetic and copies ran while one was open for 9% of the time, Pallas kernels for 0%

commit v1 on v0

--- a/solution.py
+++ b/solution.py
@@ -171,7 +171,9 @@
     own_weight_bc = lax.dynamic_slice_in_dim(conv_weight_bc, column_start, bc_width, 1)
     own_bias_bc = lax.dynamic_slice_in_dim(conv_bias_bc, column_start, bc_width, 0)
     mixed_bc_part = causal_conv(head_bc_part, own_state_bc, own_weight_bc, own_bias_bc)
-    mixed_bc = lax.all_gather(mixed_bc_part, "tj", axis=1, tiled=True)
+    mixed_bc = jnp.concatenate(
+        lax.all_to_all(jnp.stack([mixed_bc_part] * lax.axis_size("tj")), "tj", 0, 0), axis=1
+    )
     mixed_x = causal_conv(head_x, conv_state_x, conv_weight_x, conv_bias_x)
     mixed_y, final_state = state_mix(
         mixed_x, mixed_bc, head_step, step_bias, decay_rate, skip_gain, scan_state, 1

time: 249 us -> 222 us (0.89)
  the two profiles are of different devices: /device:TPU:65 before, /device:TPU:79 now
where the time goes in v1:
time: 222 us; the launch traced here: 221 us
  waiting for transfers between devices  98.2 us (44%)
  local copies, waits for them, and re-layouts  42.4 us (19%)
  matrix products  31.5 us (14%)
  starting transfers between devices  22.8 us (10%)
  other arithmetic  14.6 us (7%)
  loops' own time  10.8 us (5%)
    all_to_all x1, waiting for transfers between devices, local(): recv = lax.all_to_all(send, TENSOR, 0, 0, tiled=True)  58.2 us
    all_to_all x1, waiting for transfers between devices, local(): lax.all_to_all(mixed_y, TENSOR, split_axis=0, concat_axis=1, tiled=True)  39.5 us
    dot_general x16, matrix products, one_head(): return jnp.dot(weights, values, preferred_element_type=jnp.float32)  23.5 us
    all_to_all x1, starting transfers between devices, local(): recv = lax.all_to_all(send, TENSOR, 0, 0, tiled=True)  12.5 us
    another operation x2, loops' own time, state_mix(): lax.map(one_head, (jnp.arange(heads_here, dtype=jnp.int32), step_cols, ru...  10.8 us
    unnamed x44, local copies, waits for them, and re-layouts  9.82 us
    dynamic_slice x24, local copies, waits for them, and re-layouts, state_mix(): lax.map(one_head, (jnp.arange(heads_here, dtype=jnp.int32), step_cols, ru...  9.47 us
    all_to_all x1, starting transfers between devices, local(): lax.all_to_all(mixed_y, TENSOR, split_axis=0, concat_axis=1, tiled=True)  6.8 us
  transfers between devices with their start and end apart: 3, of which 3 were waited for; matrix products, arithmetic and copies ran while one was open for 11% of the time, Pallas kernels for 0%

profile of v1, /device:TPU:79, one launch (start us, length us, event | category | flops | bytes accessed | tf_op | source)
XLA Modules:
  0.0 221.4 jit_solution(4748677072235049546)
XLA Ops:
  0.7 0.9 copy.151
  3.4 1.7 reduce.7
  5.1 1.2 reshape.199
  6.3 12.5 %all-to-all-start = ((bf16[16,2,20736]{2,1,0:T(2,128)(2,1)}), bf16[16,2,20736]{2,1,0:T(2,128)(2,1)}, u32[]{:S(2)}, u32[]{:S(2)}) async-start(bf16[16,2,20736]{2,1,0:T(2,128)(2,1)} %reshape.199), calls=%async_computation | async-start | bytes 2654208 | tf_op jit(solution)/shard_map/all_to_all | solution.py:162
  18.8 0.8 dynamic-slice_convert_fusion.1
  19.5 0.7 constant_dynamic-slice_fusion.4
  20.2 0.7 dynamic-slice_convert_fusion
  20.9 58.2 %all-to-all-done = bf16[16,2,20736]{2,1,0:T(2,128)(2,1)} async-done(((bf16[16,2,20736]{2,1,0:T(2,128)(2,1)}), bf16[16,2,20736]{2,1,0:T(2,128)(2,1)}, u32[]{:S(2)}, u32[]{:S(2)}) %all-to-all-start) | async-done | bytes 1327136 | tf_op jit(solution)/shard_map/all_to_all | solution.py:162
  79.1 4.4 %reshape.200 = bf16[16,1,41472]{2,1,0:T(2,128)(2,1)S(1)} reshape(bf16[16,2,20736]{2,1,0:T(2,128)(2,1)} %all-to-all-done) | data formatting | bytes 2654208
  83.7 1.1 copy-done.5
  85.5 1.1 stack.2
  86.6 3.5 %all-to-all-start.1 = ((bf16[4,1024,128]{1,2,0:T(8,128)(2,1)}), bf16[4,1024,128]{1,2,0:T(8,128)(2,1)S(1)}, u32[]{:S(2)}, u32[]{:S(2)}) async-start(bf16[4,1024,128]{1,2,0:T(8,128)(2,1)} %stack.2), calls=%async_computation.1 | async-start | bytes 2097152 | tf_op jit(solution)/shard_map/all_to_all | solution.py:175
  90.4 1.0 slice.147
  91.4 2.4 %reshape.180 = bf16[1024,512]{1,0:T(8,128)(2,1)} reshape(bf16[16,32768]{1,0:T(8,128)(2,1)} %slice.147) | data formatting | bytes 2097152 | tf_op jit(solution)/shard_map/reshape | solution.py:166
  94.4 2.3 %reduce-window.6 = f32[8,8,128]{2,1,0:T(8,128)S(1)} reduce-window(f32[8,8,128]{2,1,0:T(8,128)S(1)} %copy.157, f32[]{:T(128)} %constant.83.clone.1), window={size=1x1x128 pad=0_0x0_0x127_0}, to_apply=%region_0.1 | reduce-window | flops 1040384 | bytes 65540 | tf_op jit(solution)/shard_map/reduce-window
  97.4 1.4 multiply_convert_fusion.3
  99.1 1.6 mul.280
  100.7 2.9 %copy.162 = f32[1024,512]{1,0:T(8,128)} copy(f32[1024,512]{0,1:T(8,128)} %bitcast.181) | data formatting | bytes 4194304 | tf_op jit(solution)/shard_map/mul | solution.py:92
  104.4 1.8 convolution_bitcast_fusion.2
  106.3 13.6 %while.24 = (s32[]{:T(128)}, f32[8,512,64]{1,2,0:T(8,128)S(1)}, f32[1,512,512]{2,1,0:T(8,128)S(1)}, f32[8,1024]{1,0:T(8,128)S(1)}, f32[8,1024]{1,0:T(8,128)S(1)}...) while((s32[]{:T(128)}, f32[8,512,64]{1,2,0:T(8,128)S(1)}, ...), condition=%wide.region_3.4_spmd.clone.clone, body=%wide.region_2.3_spmd.clone.clone.sunk | while | flops 35389444 | bytes 1325243 | solution.py:78
  106.3 0.6 dynamic_slice.73
  108.0 0.6 dynamic_slice.73
  111.4 0.6 dynamic_slice.73
  113.1 0.6 dynamic_slice.73
  114.8 0.6 dynamic_slice.73
  119.9 1.4 copy.158
  121.3 30.9 %while.25 = (s32[]{:T(128)}, f32[8,512,64]{1,2,0:T(8,128)S(1)}, f32[1,512,1024]{2,1,0:T(8,128)}, f32[8,1024]{1,0:T(8,128)S(1)}, f32[8,1024]{1,0:T(8,128)S(1)}, /...) while((s32[]{:T(128)}, f32[8,512,64]{1,2,0:T(8,128)S(1)}, ...), condition=%wide.region_5.6_spmd.clone.clone, body=%wide.region_4.5_spmd.clone.clone.sunk | while | flops 70778888 | bytes 2523355 | solution.py:78
  122.7 2.5 %fusion.71 = f32[8,512,64]{1,2,0:T(8,128)S(1)} fusion(f32[8,512,64]{1,2,0:T(8,128)S(1)} %get-tuple-element.426, s32[]{:T(128)S(6)} %copy.196, f32[1,512,1024]{2,1,0:T(8,128)} %get-tuple-element.440, s32[512]{0:T(512)S(1)} %get-tuple-element.445, f32[1024]{0:T(1024)S(1)} %bitcast.199, f32[1024]{0:T(1024)S(1)} %bitcast.200, f32[512]{0:T(512)S(1)} %bitcast.203, ...), kind=kOutput, calls=%fused_computation.28.clone.1 | convolution fusion | flops 70778880 | bytes 2502664 | tf_op jit(solution)/shard_map/while/body/eval_jaxpr/dot_general | solution.py:76
  126.6 2.5 %fusion.71 = f32[8,512,64]{1,2,0:T(8,128)S(1)} fusion(f32[8,512,64]{1,2,0:T(8,128)S(1)} %get-tuple-element.426, s32[]{:T(128)S(6)} %copy.196, f32[1,512,1024]{2,1,0:T(8,128)} %get-tuple-element.440, s32[512]{0:T(512)S(1)} %get-tuple-element.445, f32[1024]{0:T(1024)S(1)} %bitcast.199, f32[1024]{0:T(1024)S(1)} %bitcast.200, f32[512]{0:T(512)S(1)} %bitcast.203, ...), kind=kOutput, calls=%fused_computation.28.clone.1 | convolution fusion | flops 70778880 | bytes 2502664 | tf_op jit(solution)/shard_map/while/body/eval_jaxpr/dot_general | solution.py:76
  130.4 2.5 %fusion.71 = f32[8,512,64]{1,2,0:T(8,128)S(1)} fusion(f32[8,512,64]{1,2,0:T(8,128)S(1)} %get-tuple-element.426, s32[]{:T(128)S(6)} %copy.196, f32[1,512,1024]{2,1,0:T(8,128)} %get-tuple-element.440, s32[512]{0:T(512)S(1)} %get-tuple-element.445, f32[1024]{0:T(1024)S(1)} %bitcast.199, f32[1024]{0:T(1024)S(1)} %bitcast.200, f32[512]{0:T(512)S(1)} %bitcast.203, ...), kind=kOutput, calls=%fused_computation.28.clone.1 | convolution fusion | flops 70778880 | bytes 2502664 | tf_op jit(solution)/shard_map/while/body/eval_jaxpr/dot_general | solution.py:76
  134.3 2.5 %fusion.71 = f32[8,512,64]{1,2,0:T(8,128)S(1)} fusion(f32[8,512,64]{1,2,0:T(8,128)S(1)} %get-tuple-element.426, s32[]{:T(128)S(6)} %copy.196, f32[1,512,1024]{2,1,0:T(8,128)} %get-tuple-element.440, s32[512]{0:T(512)S(1)} %get-tuple-element.445, f32[1024]{0:T(1024)S(1)} %bitcast.199, f32[1024]{0:T(1024)S(1)} %bitcast.200, f32[512]{0:T(512)S(1)} %bitcast.203, ...), kind=kOutput, calls=%fused_computation.28.clone.1 | convolution fusion | flops 70778880 | bytes 2502664 | tf_op jit(solution)/shard_map/while/body/eval_jaxpr/dot_general | solution.py:76
  138.2 2.5 %fusion.71 = f32[8,512,64]{1,2,0:T(8,128)S(1)} fusion(f32[8,512,64]{1,2,0:T(8,128)S(1)} %get-tuple-element.426, s32[]{:T(128)S(6)} %copy.196, f32[1,512,1024]{2,1,0:T(8,128)} %get-tuple-element.440, s32[512]{0:T(512)S(1)} %get-tuple-element.445, f32[1024]{0:T(1024)S(1)} %bitcast.199, f32[1024]{0:T(1024)S(1)} %bitcast.200, f32[512]{0:T(512)S(1)} %bitcast.203, ...), kind=kOutput, calls=%fused_computation.28.clone.1 | convolution fusion | flops 70778880 | bytes 2502664 | tf_op jit(solution)/shard_map/while/body/eval_jaxpr/dot_general | solution.py:76
  142.0 2.5 %fusion.71 = f32[8,512,64]{1,2,0:T(8,128)S(1)} fusion(f32[8,512,64]{1,2,0:T(8,128)S(1)} %get-tuple-element.426, s32[]{:T(128)S(6)} %copy.196, f32[1,512,1024]{2,1,0:T(8,128)} %get-tuple-element.440, s32[512]{0:T(512)S(1)} %get-tuple-element.445, f32[1024]{0:T(1024)S(1)} %bitcast.199, f32[1024]{0:T(1024)S(1)} %bitcast.200, f32[512]{0:T(512)S(1)} %bitcast.203, ...), kind=kOutput, calls=%fused_computation.28.clone.1 | convolution fusion | flops 70778880 | bytes 2502664 | tf_op jit(solution)/shard_map/while/body/eval_jaxpr/dot_general | solution.py:76
  145.9 2.5 %fusion.71 = f32[8,512,64]{1,2,0:T(8,128)S(1)} fusion(f32[8,512,64]{1,2,0:T(8,128)S(1)} %get-tuple-element.426, s32[]{:T(128)S(6)} %copy.196, f32[1,512,1024]{2,1,0:T(8,128)} %get-tuple-element.440, s32[512]{0:T(512)S(1)} %get-tuple-element.445, f32[1024]{0:T(1024)S(1)} %bitcast.199, f32[1024]{0:T(1024)S(1)} %bitcast.200, f32[512]{0:T(512)S(1)} %bitcast.203, ...), kind=kOutput, calls=%fused_computation.28.clone.1 | convolution fusion | flops 70778880 | bytes 2502664 | tf_op jit(solution)/shard_map/while/body/eval_jaxpr/dot_general | solution.py:76
  149.8 2.5 %fusion.71 = f32[8,512,64]{1,2,0:T(8,128)S(1)} fusion(f32[8,512,64]{1,2,0:T(8,128)S(1)} %get-tuple-element.426, s32[]{:T(128)S(6)} %copy.196, f32[1,512,1024]{2,1,0:T(8,128)} %get-tuple-element.440, s32[512]{0:T(512)S(1)} %get-tuple-element.445, f32[1024]{0:T(1024)S(1)} %bitcast.199, f32[1024]{0:T(1024)S(1)} %bitcast.200, f32[512]{0:T(512)S(1)} %bitcast.203, ...), kind=kOutput, calls=%fused_computation.28.clone.1 | convolution fusion | flops 70778880 | bytes 2502664 | tf_op jit(solution)/shard_map/while/body/eval_jaxpr/dot_general | solution.py:76
  152.3 1.3 copy.159
  153.6 2.2 fusion.52
  155.8 1.8 copy.161
  157.6 4.7 %fusion.42 = bf16[1024,512]{1,0:T(8,128)(2,1)} fusion(f32[512,512]{1,0:T(8,128)} %copy.159, f32[512,512]{1,0:T(8,128)} %copy.158, bf16[1024,512]{1,0:T(8,128)(2,1)S(1)} %get-tuple-element.484, f32[1024,512]{1,0:T(8,128)} %copy.161, f32[1024,512]{1,0:T(8,128)} %copy.162, f32[512]{0:T(512)S(1)} %mul.284), kind=kLoop, calls=%fused_computation.55 | loop fusion | flops 3670016 | bytes 8390656 | tf_op jit(solution)/shard_map/convert_element_type | solution.py:99
  162.4 6.8 %all-to-all-start.2 = ((bf16[16,64,512]{2,1,0:T(8,128)(2,1)}), bf16[16,64,512]{2,1,0:T(8,128)(2,1)S(1)}, u32[]{:S(2)}, u32[]{:S(2)}) async-start(bf16[16,64,512]{2,1,0:T(8,128)(2,1)} %bitcast.186), calls=%async_computation.2 | async-start | bytes 2097152 | tf_op jit(solution)/shard_map/all_to_all | solution.py:181
  169.2 1.3 slice.158
  170.4 1.3 slice.157
  171.7 1.3 copy.165
  173.2 1.3 copy.166
  174.5 3.8 %fusion.43 = f32[8,64,256]{2,1,0:T(8,128)} fusion(bf16[1024,8,64]{0,2,1:T(8,128)(2,1)} %bitcast.192, f32[1024,8]{0,1:T(8,128)S(1)} %get-tuple-element.299, f32[1024,256]{1,0:T(8,128)} %copy.166, f32[8,64,256]{2,1,0:T(8,128)S(1)} %copy-done.8, f32[8]{0:T(128)S(1)} %exp.35), kind=kOutput, calls=%fused_computation.62 | convolution fusion | flops 272891904 | bytes 3178528 | tf_op jit(solution)/shard_map/tghp,tghn->ghpn/dot_general | solution.py:105
  178.2 39.5 %all-to-all-done.2 = bf16[16,64,512]{2,1,0:T(8,128)(2,1)S(1)} async-done(((bf16[16,64,512]{2,1,0:T(8,128)(2,1)}), bf16[16,64,512]{2,1,0:T(8,128)(2,1)S(1)}, u32[]{:S(2)}, u32[]{:S(2)}) %all-to-all-start.2) | async-done | bytes 1048608 | tf_op jit(solution)/shard_map/all_to_all | solution.py:181
  219.0 1.2 copy.175
  220.2 1.2 multiply_convert_fusion.2
  (129 shorter events, 17.4 us)
Async XLA Ops:
  0.6 1.2 copy-start
  0.6 1.4 copy-start.10
  6.3 72.8 %all-to-all-start = ((bf16[16,2,20736]{2,1,0:T(2,128)(2,1)}), bf16[16,2,20736]{2,1,0:T(2,128)(2,1)}, u32[]{:S(2)}, u32[]{:S(2)}) async-start(bf16[16,2,20736]{2,1,0:T(2,128)(2,1)} %reshape.199), calls=%async_computation | async-start | bytes 2654208 | tf_op jit(solution)/shard_map/all_to_all | solution.py:162
  83.7 1.1 copy-start.5
  84.9 1.7 copy-start.9
  85.3 4.8 %copy-start.15 = (bf16[512]{0:T(512)(128)(2,1)S(1)}, bf16[512]{0:T(512)(128)(2,1)}, u32[]{:S(2)}) copy-start(bf16[512]{0:T(512)(128)(2,1)} %param.24) | copy-start | bytes 3076
  85.3 4.8 %copy-start.17 = (f32[8]{0:T(128)S(1)}, f32[8]{0:T(128)}, u32[]{:S(2)}) copy-start(f32[8]{0:T(128)} %param.29) | copy-start | bytes 100
  85.4 5.0 %copy-start.13 = (bf16[3,512]{1,0:T(4,128)(2,1)S(1)}, bf16[3,512]{1,0:T(4,128)(2,1)}, u32[]{:S(2)}) copy-start(bf16[3,512]{1,0:T(4,128)(2,1)} %param.21) | copy-start | bytes 9220
  85.4 5.0 %copy-start.12 = (bf16[4,512]{1,0:T(4,128)(2,1)S(1)}, bf16[4,512]{1,0:T(4,128)(2,1)}, u32[]{:S(2)}) copy-start(bf16[4,512]{1,0:T(4,128)(2,1)} %param.23) | copy-start | bytes 12292
  85.4 5.0 %copy-start.6 = (bf16[16,1,41472]{2,0,1:T(8,128)(2,1)S(1)}, bf16[16,1,41472]{2,0,1:T(8,128)(2,1)}, u32[]{:S(2)}) copy-start(bf16[16,1,41472]{2,0,1:T(8,128)(2,1)} %copy-done.5) | copy-start | bytes 3981316
  86.6 17.4 %all-to-all-start.1 = ((bf16[4,1024,128]{1,2,0:T(8,128)(2,1)}), bf16[4,1024,128]{1,2,0:T(8,128)(2,1)S(1)}, u32[]{:S(2)}, u32[]{:S(2)}) async-start(bf16[4,1024,128]{1,2,0:T(8,128)(2,1)} %stack.2), calls=%async_computation.1 | async-start | bytes 2097152 | tf_op jit(solution)/shard_map/all_to_all | solution.py:175
  91.4 2.9 %copy-start.14 = (f32[8]{0:T(128)S(1)}, f32[8]{0:T(128)}, u32[]{:S(2)}) copy-start(f32[8]{0:T(128)} %param.27) | copy-start | bytes 100
  91.4 2.9 %copy-start.16 = (f32[8]{0:T(128)S(1)}, f32[8]{0:T(128)}, u32[]{:S(2)}) copy-start(f32[8]{0:T(128)} %param.28) | copy-start | bytes 100
  93.8 3.3 %copy-start.7 = (bf16[1024,512]{1,0:T(8,128)(2,1)S(1)}, bf16[1024,512]{1,0:T(8,128)(2,1)}, u32[]{:S(2)}) copy-start(bf16[1024,512]{1,0:T(8,128)(2,1)} %reshape.180) | copy-start | bytes 3145732
  98.8 4.8 %copy-start.1 = (bf16[1024,512]{1,0:T(8,128)(2,1)}, bf16[1024,512]{1,0:T(8,128)(2,1)S(1)}, u32[]{:S(2)}) copy-start(bf16[1024,512]{1,0:T(8,128)(2,1)S(1)} %multiply_convert_fusion.3) | copy-start | bytes 3145732
  104.0 2.1 copy-start.3
  104.3 1.9 slice-start
  119.8 1.5 copy-start.2
  162.4 6.8 %copy-start.11 = (bf16[8192]{0:T(1024)(128)(2,1)S(1)}, bf16[8192]{0:T(1024)(128)(2,1)}, u32[]{:S(2)}) copy-start(bf16[8192]{0:T(1024)(128)(2,1)} %param.30) | copy-start | bytes 49156
  162.4 10.7 %copy-start.4 = (bf16[4,1024,128]{1,2,0:T(8,128)(2,1)S(1)}, bf16[4,1024,128]{1,2,0:T(8,128)(2,1)}, u32[]{:S(2)}) copy-start(bf16[4,1024,128]{1,2,0:T(8,128)(2,1)} %copy-done.3) | copy-start | bytes 3145732
  162.4 55.4 %all-to-all-start.2 = ((bf16[16,64,512]{2,1,0:T(8,128)(2,1)}), bf16[16,64,512]{2,1,0:T(8,128)(2,1)S(1)}, u32[]{:S(2)}, u32[]{:S(2)}) async-start(bf16[16,64,512]{2,1,0:T(8,128)(2,1)} %bitcast.186), calls=%async_computation.2 | async-start | bytes 2097152 | tf_op jit(solution)/shard_map/all_to_all | solution.py:181
  173.2 1.3 copy-start.8
